TPU v7x, 32 devices: a whole 2x2x4 slice. The times are simulated.
32 devices in a mesh: grp: 2 (over y), ctx: 8 (over z, x), pair: 2 (over core).
Axes of the slice: x: 2, y: 2, z: 4, core: 2. Of those that a mesh axis runs over, the one named last changes fastest.
Arguments:
- normed_input: bfloat16 [4, 1024, 2688], P(('grp', 'pair'), 'ctx'), parts along dimension 0, may hold values from -6 to 6
- queries: bfloat16 [4, 1024, 2048], P(('grp', 'pair'), 'ctx'), parts along dimension 0, may hold values from -64 to 64
- keys: bfloat16 [4, 1024, 1024], P(('grp', 'pair'), 'ctx'), parts along dimension 0, may hold values from -64 to 64
- value_projection: bfloat16 [2688, 1024], P('ctx'), may hold values from -0.125 to 0.125
- adapter_down: bfloat16 [2688, 16], replicated, may hold values from -0.125 to 0.125
- adapter_up: bfloat16 [16, 1024], replicated, may hold values from -1.5 to 1.5
- output_gradient: bfloat16 [4, 1024, 2048], P(('grp', 'pair'), 'ctx'), parts along dimension 0, may hold values from -6 to 6
- policy_logprob: float32 [4, 1024], P(('grp', 'pair'), 'ctx'), parts along dimension 0, may hold values from -6 to 0
- reference_logprob: float32 [4, 1024], P(('grp', 'pair'), 'ctx'), parts along dimension 0, may hold values from -8 to 0
- token_pair_index: int32 [4, 1024], P(('grp', 'pair'), 'ctx'), parts along dimension 0, may hold values from 0 to 7, never falling along the last dimension, each value on 1 to 1017 neighbouring positions
Outputs:
- input_grad: bfloat16 [4, 1024, 2688], P(('grp', 'pair'), 'ctx'), parts along dimension 0
- query_grad: bfloat16 [4, 1024, 2048], P(('grp', 'pair'), 'ctx'), parts along dimension 0
- key_grad: bfloat16 [4, 1024, 1024], P(('grp', 'pair'), 'ctx'), parts along dimension 0
- down_gradient: float32 [5376, 16], P('grp'), parts along dimension 0
- up_gradient: float32 [32, 1024], P('grp'), parts along dimension 0
There are 2 independent parts, one for each index of `grp`. A program takes and returns all parts, laid end to end along the dimension named above; an argument that names none is the same for every part. Nothing has to cross between parts.
Inputs may be any that keep to these rules, and one draw needn't show every extreme that they name: `token_pair_index`: along each sequence the ids never fall; both sequences hold every id, each segment at most 1017 tokens and one exactly 1017.
All inputs are finite; a program needn't handle non-finite values.
Results may differ from a plain program's by a relative error of at most 0.03.
Values may be sent and summed in bfloat16 or wider, within the bound.
No kernel may reach another device: no remote copies, remote signals or barrier semaphores. Data moves between devices by JAX's collectives and lax.ppermute only.
A program may use at most 128 MiB of HBM per device.

v0:
```python
import jax
import jax.numpy as jnp
from jax import lax
from jax.sharding import PartitionSpec as P

HEAD_SIZE = 128
WINDOW = 1024
SEGS = 8
DPO_BETA = 0.1
LOSS_SCALE = 256.0
ADAPTER_SCALE = 2.0
ATTN_SCALE = 168.0 ** (-0.5)
NEG_FILL = -1e30


def from_partner(shard, axis, stride):
    return lax.ppermute(shard, axis, [(i, i ^ 1 << stride) for i in range(lax.axis_size(axis))])


def shifted(block, axis, distance):
    devices = range(lax.axis_size(axis))
    route = [(i - distance, i) for i in devices if i - distance in devices]
    return lax.ppermute(block, axis, route)


def shards(
    normed_input,
    queries,
    keys,
    value_projection,
    adapter_down,
    adapter_up,
    output_gradient,
    policy_logprob,
    reference_logprob,
    token_pair_index,
):
    tok_rows = normed_input.shape[1]
    width_kv = keys.shape[2]
    kv_heads = width_kv // HEAD_SIZE
    group_size = queries.shape[2] // width_kv
    hidden_rows = normed_input[0]
    own_keys = keys[0]
    pair_index = lax.axis_index("pair")
    ctx_index = lax.axis_index("ctx")
    half_cols = width_kv // 2
    own_half = lax.dynamic_slice_in_dim(value_projection, pair_index * half_cols, half_cols, 1)
    rows_half = lax.all_gather(own_half, "ctx", axis=0, tiled=True)
    full_weight = lax.all_gather(rows_half, "pair", axis=1, tiled=True)
    rank_projection = jnp.dot(hidden_rows, adapter_down, preferred_element_type=jnp.float32).astype(
        jnp.bfloat16
    )
    values = (
        jnp.dot(hidden_rows, full_weight, preferred_element_type=jnp.float32)
        + ADAPTER_SCALE * jnp.dot(rank_projection, adapter_up, preferred_element_type=jnp.float32)
    ).astype(jnp.bfloat16)
    segment_labels = token_pair_index[0]
    seg_table = (segment_labels[:, None] == jnp.arange(SEGS, dtype=jnp.int32)[None, :]).astype(
        jnp.float32
    )
    log_gap = policy_logprob[0] - reference_logprob[0]
    part_diff = jnp.sum(seg_table * log_gap[:, None], 0)
    part_count = jnp.sum(seg_table, 0)
    own_diff, counts = lax.psum((part_diff, part_count), "ctx")
    other_diff = from_partner(own_diff, "pair", 0)
    direction = 1.0 - 2.0 * pair_index.astype(jnp.float32)
    margin = DPO_BETA * (direction * (own_diff - other_diff))
    coef = -direction * DPO_BETA * LOSS_SCALE * jax.nn.sigmoid(-margin)
    starts = jnp.cumsum(counts) - counts
    tok_start = jnp.sum(seg_table * starts[None, :], 1).astype(jnp.int32)
    token_coefficient = jnp.sum(seg_table * coef[None, :], 1)
    halo_blocks = min(WINDOW // tok_rows, lax.axis_size("ctx") - 1)
    key_blocks = []
    value_blocks = []
    for distance in range(halo_blocks, 0, -1):
        key_blocks.append(shifted(own_keys, "ctx", distance))
        value_blocks.append(shifted(values, "ctx", distance))
    all_keys = jnp.concatenate(key_blocks + [own_keys], 0)
    all_keys, own_values = lax.optimization_barrier((all_keys, values))
    all_values = jnp.concatenate(value_blocks + [own_values], 0)
    span = all_keys.shape[0]
    tpos = ctx_index * tok_rows + jnp.arange(tok_rows, dtype=jnp.int32)
    upos = ctx_index * tok_rows - halo_blocks * tok_rows + jnp.arange(span, dtype=jnp.int32)
    allowed = (
        (upos[None, :] <= tpos[:, None])
        & (upos[None, :] > tpos[:, None] - WINDOW)
        & (upos[None, :] >= tok_start[:, None])
    )
    coef_rows = token_coefficient[None, :, None]
    query_rows = queries[0].reshape(tok_rows, kv_heads, group_size, HEAD_SIZE)
    grad_rows = output_gradient[0].reshape(tok_rows, kv_heads, group_size, HEAD_SIZE)
    key_rows = all_keys.reshape(span, kv_heads, HEAD_SIZE)
    value_rows = all_values.reshape(span, kv_heads, HEAD_SIZE)
    scores = ATTN_SCALE * jnp.einsum(
        "tjgd,ljd->jgtl", query_rows, key_rows, preferred_element_type=jnp.float32
    )
    masked = jnp.where(allowed[None, None], scores, NEG_FILL)
    row_max = jnp.max(masked, -1, keepdims=True)
    weights_exp = jnp.where(allowed[None, None], jnp.exp(masked - row_max), 0.0)
    attn_probs = weights_exp / jnp.sum(weights_exp, -1, keepdims=True)
    prob_grad = coef_rows[None] * jnp.einsum(
        "tjgd,ljd->jgtl", grad_rows, value_rows, preferred_element_type=jnp.float32
    )
    row_delta = jnp.sum(attn_probs * prob_grad, -1, keepdims=True)
    score_grad = (ATTN_SCALE * attn_probs * (prob_grad - row_delta)).astype(jnp.bfloat16)
    query_grad = (
        jnp.einsum("jgtl,ljd->tjgd", score_grad, key_rows, preferred_element_type=jnp.float32)
        .astype(jnp.bfloat16)
        .reshape(tok_rows, kv_heads * group_size * HEAD_SIZE)
    )
    key_parts = jnp.einsum(
        "jgtl,tjgd->ljd", score_grad, query_rows, preferred_element_type=jnp.float32
    ).reshape(span, width_kv)
    weighted = (attn_probs * coef_rows[None]).astype(jnp.bfloat16)
    value_parts = jnp.einsum(
        "jgtl,tjgd->ljd", weighted, grad_rows, preferred_element_type=jnp.float32
    ).reshape(span, width_kv)
    key_total = key_parts[halo_blocks * tok_rows :]
    value_total = value_parts[halo_blocks * tok_rows :]
    for distance in range(1, halo_blocks + 1):
        block_start = (halo_blocks - distance) * tok_rows
        send_keys = key_parts[block_start : block_start + tok_rows].astype(jnp.bfloat16)
        send_values = value_parts[block_start : block_start + tok_rows].astype(jnp.bfloat16)
        back_keys, back_values = shifted((send_keys, send_values), "ctx", -distance)
        key_total = key_total + back_keys.astype(jnp.float32)
        value_total = value_total + back_values.astype(jnp.float32)
    key_grad = key_total.astype(jnp.bfloat16)
    value_gradient = value_total.astype(jnp.bfloat16)
    rank_middle = jnp.einsum(
        "sj,zj->sz", value_gradient, adapter_up, preferred_element_type=jnp.float32
    ).astype(jnp.bfloat16)
    input_grad = (
        jnp.einsum("tk,dk->td", value_gradient, full_weight, preferred_element_type=jnp.float32)
        + ADAPTER_SCALE
        * jnp.einsum("pb,wb->pw", rank_middle, adapter_down, preferred_element_type=jnp.float32)
    ).astype(jnp.bfloat16)
    up_factor = ADAPTER_SCALE * jnp.einsum(
        "tr,tk->rk", rank_projection, value_gradient, preferred_element_type=jnp.float32
    )
    down_factor = ADAPTER_SCALE * jnp.einsum(
        "td,tr->dr", hidden_rows, rank_middle, preferred_element_type=jnp.float32
    )
    down_gradient, up_gradient = lax.psum((down_factor, up_factor), ("ctx", "pair"))
    return (input_grad[None], query_grad[None], key_grad[None], down_gradient, up_gradient)


def solution(mesh):
    return jax.shard_map(
        shards,
        mesh=mesh,
        in_specs=(
            P(("grp", "pair"), "ctx", None),
            P(("grp", "pair"), "ctx", None),
            P(("grp", "pair"), "ctx", None),
            P("ctx", None),
            P(),
            P(),
            P(("grp", "pair"), "ctx", None),
            P(("grp", "pair"), "ctx"),
            P(("grp", "pair"), "ctx"),
            P(("grp", "pair"), "ctx"),
        ),
        out_specs=(
            P(("grp", "pair"), "ctx", None),
            P(("grp", "pair"), "ctx", None),
            P(("grp", "pair"), "ctx", None),
            P("grp", None),
            P("grp", None),
        ),
        check_vma=False,
    )
```

profile of v0, /device:TPU:8, one launch (start us, length us, event | category | flops | bytes accessed | tf_op | source)
XLA Modules:
  0.0 361.4 jit_solution(16586474015925666652)
XLA Ops:
  7.3 1.8 constant_dynamic-slice_fusion
  9.2 58.9 %all-gather.3.cloned.1.call-done = bf16[2688,512]{1,0:T(8,128)(2,1)} async-done(((bf16[336,512]{1,0:T(8,128)(2,1)}), bf16[2688,512]{1,0:T(8,128)(2,1)}) %all-gather.3.cloned.1.call-update) | async-done | bytes 2752528 | tf_op jit(solution)/shard_map/all_gather | solution.py:48
  68.8 1.4 collective-permute-start.1
  70.2 4.2 %collective-permute-start.2 = (bf16[128,1024]{1,0:T(8,128)(2,1)}, bf16[128,1024]{1,0:T(8,128)(2,1)}, u32[]{:S(2)}, u32[]{:S(2)}) collective-permute-start(bf16[128,1024]{1,0:T(8,128)(2,1)} %bitcast.3), channel_id=1, source_target_pairs={{0,10},{2,12},{4,14},{1,11},{3,13},{5,15},{16,26},{18,28},{20,30},... | collective-permute-start | bytes 786440 | tf_op jit(solution)/shard_map/ppermute | solution.py:23
  74.3 2.0 collective-permute-start.3
  76.5 30.3 %all-reduce.1 = (f32[8]{0:T(128)S(1)}, f32[8]{0:T(128)S(1)}) all-reduce(f32[8]{0:T(128)S(1)} %get-tuple-element.21, f32[8]{0:T(128)S(1)} %get-tuple-element.22), channel_id=1, replica_groups=mesh['grp'=2,'ctx'=8,'pair'=2] {'ctx'}, use_global_device_ids=true, to_apply=%region_1.0 | all-reduce | flops 16 | bytes 128 | tf_op jit(solution)/shard_map/psum | solution.py:64
  108.8 2.9 collective-permute-start.4
  113.4 3.2 collective-permute-start.5
  117.5 1.9 collective-permute-start.6
  122.4 3.8 %collective-permute-done.5 = bf16[128,1024]{1,0:T(8,128)(2,1)S(1)} collective-permute-done((bf16[128,1024]{1,0:T(8,128)(2,1)}, bf16[128,1024]{1,0:T(8,128)(2,1)S(1)}, u32[]{:S(2)}, u32[]{:S(2)}) %collective-permute-start.5) | collective-permute-done | bytes 262176 | tf_op jit(solution)/shard_map/ppermute | solution.py:23
  126.3 4.2 %collective-permute-done.6 = bf16[128,1024]{1,0:T(8,128)(2,1)S(1)} collective-permute-done((bf16[128,1024]{1,0:T(8,128)(2,1)}, bf16[128,1024]{1,0:T(8,128)(2,1)S(1)}, u32[]{:S(2)}, u32[]{:S(2)}) %collective-permute-start.6) | collective-permute-done | bytes 262176 | tf_op jit(solution)/shard_map/ppermute | solution.py:23
  131.5 4.2 %convolution_bitcast_fusion.1 = f32[128,1024]{0,1:T(8,128)S(1)} fusion(bf16[2688,1024]{1,0:T(8,128)(2,1)} %all-gather.5.cloned.1.call-done, bf16[1,128,2688]{2,1,0:T(8,128)(2,1)S(1)} %copy-done), kind=kOutput, calls=%fused_computation.26 | convolution fusion | flops 704643072 | bytes 6717440 | tf_op jit(solution)/shard_map/dot_general | solution.py:54
  136.7 1.3 collective-permute-start.15
  138.0 1.4 collective-permute-start.16
  139.4 2.3 collective-permute-start.17
  141.6 6.5 %collective-permute-start.18 = (bf16[128,1024]{0,1:T(8,128)(2,1)}, bf16[128,1024]{0,1:T(8,128)(2,1)}, u32[]{:S(2)}, u32[]{:S(2)}) collective-permute-start(bf16[128,1024]{0,1:T(8,128)(2,1)} %fusion.15), channel_id=1, source_target_pairs={{0,8},{2,10},{4,12},{6,14},{1,9},{3,11},{5,13},{7,15},{16,24},{18,... | collective-permute-start | bytes 786440 | tf_op jit(solution)/shard_map/ppermute | solution.py:23
  148.2 2.0 collective-permute-start.19
  150.2 2.0 copy.71
  152.1 3.2 copy.60
  155.4 6.9 %fusion.36 = (f32[8,2,128]{2,1,0:T(2,128)S(1)}, f32[8,2,128,1024]{2,3,1,0:T(8,128)}) fusion(pred[128,1024]{0,1:T(8,128)(4,1)} %compare_and_fusion, bf16[1024,8,128,1]{0,2,3,1:T(8,128)(2,1)S(1)} %copy.60, bf16[128,8,2,128]{0,3,2,1:T(8,128)(2,1)S(1)} %bitcast.126), kind=kOutput, calls=%fused_computation.82 | convolution fusion | flops 547357696 | bytes 11149312 | tf_op jit(solution)/shard_map/sub | solution.py:99
  162.3 5.1 %fusion.37 = (bf16[1024,8,128]{0,2,1:T(8,128)(2,1)S(1)}, f32[1024,8,128]{0,2,1:T(8,128)S(1)}) fusion(bf16[128,8,2,128]{3,2,1,0:T(2,128)(2,1)} %reshape_squeeze.7, f32[128]{0:T(128)S(1)} %get-tuple-element.20, f32[8,2,128,1024]{2,3,1,0:T(8,128)} %get-tuple-element.42, f32[8,2,128]{2,1,0:T(2,128)S(1)} %get-tuple-element.41), kind=kOutput, calls=%fused_computation.83 | convolution fusion | flops 544210944 | bytes 15213056 | tf_op jit(solution)/shard_map/jgtl,tjgd->ljd/dot_general | solution.py:115
  168.0 2.9 collective-permute-start.20
  172.0 1.9 collective-permute-start.21
  178.4 1.3 collective-permute-start.12
  180.8 3.2 collective-permute-done.20
  185.5 1.5 collective-permute-start.10
  188.1 1.9 fusion.1
  190.0 1.7 fusion.3
  191.8 1.6 convolution_convert_fusion
  193.4 2.9 collective-permute-start.9
  196.3 3.1 collective-permute-start.8
  199.5 3.5 fusion.38
  203.1 19.5 %collective-permute-done.10 = bf16[128,1024]{0,1:T(8,128)(2,1)S(1)} collective-permute-done((bf16[128,1024]{0,1:T(8,128)(2,1)S(1)}, bf16[128,1024]{0,1:T(8,128)(2,1)S(1)}, u32[]{:S(2)}, u32[]{:S(2)}) %collective-permute-start.10) | collective-permute-done | bytes 262176 | tf_op jit(solution)/shard_map/ppermute | solution.py:23
  222.7 1.5 collective-permute-done.9
  225.4 2.0 copy.54
  227.4 1.4 fusion.34
  228.8 1.9 copy.53
  231.4 1.8 copy.52
  233.9 1.8 copy.51
  245.5 1.9 collective-permute-start.23
  247.4 1.9 collective-permute-start.22
  249.4 5.3 %fusion.11 = bf16[1,128,2688]{2,1,0:T(8,128)(2,1)} fusion(f32[128,2688]{1,0:T(8,128)S(1)} %convolution_multiply_fusion, bf16[128,1024]{0,1:T(8,128)(2,1)S(1)} %fusion.27, bf16[2688,1024]{1,0:T(8,128)(2,1)} %all-gather.5.cloned.1.call-done), kind=kOutput, calls=%fused_computation.19 | convolution fusion | flops 705331200 | bytes 7831552 | tf_op jit(solution)/shard_map/tk,dk->td/dot_general | solution.py:133
  254.7 16.3 %collective-permute-done.24 = bf16[128,1024]{1,0:T(8,128)(2,1)} collective-permute-done((bf16[128,1024]{1,0:T(8,128)(2,1)}, bf16[128,1024]{1,0:T(8,128)(2,1)}, u32[]{:S(2)}, u32[]{:S(2)}) %collective-permute-start.24) | collective-permute-done | bytes 262176 | tf_op jit(solution)/shard_map/ppermute | solution.py:23
  271.1 3.9 %collective-permute-done.23 = bf16[128,1024]{1,0:T(8,128)(2,1)S(1)} collective-permute-done((bf16[128,1024]{1,0:T(8,128)(2,1)}, bf16[128,1024]{1,0:T(8,128)(2,1)S(1)}, u32[]{:S(2)}, u32[]{:S(2)}) %collective-permute-start.23) | collective-permute-done | bytes 262176 | tf_op jit(solution)/shard_map/ppermute | solution.py:23
  275.0 2.0 fusion.31
  277.0 74.8 %all-reduce.4.cloned.1.call-done = (f32[2688,16]{0,1:T(8,128)}, f32[16,1024]{1,0:T(8,128)}) async-done(((f32[2688,16]{0,1:T(8,128)}, f32[16,1024]{1,0:T(8,128)}), (f32[2688,16]{0,1:T(8,128)}, f32[16,1024]{1,0:T(8,128)})) %all-reduce.4.cloned.1.call-update) | async-done | bytes 237584 | tf_op jit(solution)/shard_map/psum | solution.py:143
  351.8 1.6 copy.96
  353.4 1.5 copy.97
  (113 shorter events, 32.8 us)
Async XLA Ops:
  7.2 101.3 %copy-start = (bf16[1,128,2688]{2,1,0:T(8,128)(2,1)S(1)}, bf16[1,128,2688]{2,1,0:T(8,128)(2,1)}, u32[]{:S(2)}) copy-start(bf16[1,128,2688]{2,1,0:T(8,128)(2,1)} %param.10) | copy-start | bytes 2064388
  7.2 69.2 %copy-start.11 = (f32[1,128]{1,0:T(1,128)S(1)}, f32[1,128]{1,0:T(1,128)}, u32[]{:S(2)}) copy-start(f32[1,128]{1,0:T(1,128)} %param.17) | copy-start | bytes 1540
  7.2 69.1 %copy-start.12 = (f32[1,128]{1,0:T(1,128)S(1)}, f32[1,128]{1,0:T(1,128)}, u32[]{:S(2)}) copy-start(f32[1,128]{1,0:T(1,128)} %param.18) | copy-start | bytes 1540
  7.2 69.1 %copy-start.10 = (s32[1,128]{1,0:T(1,128)S(1)}, s32[1,128]{1,0:T(1,128)}, u32[]{:S(2)}) copy-start(s32[1,128]{1,0:T(1,128)} %param.19) | copy-start | bytes 1540
  7.2 99.6 %copy-start.4 = (bf16[1,128,2048]{2,1,0:T(8,128)(2,1)S(1)}, bf16[1,128,2048]{2,1,0:T(8,128)(2,1)}, u32[]{:S(2)}) copy-start(bf16[1,128,2048]{2,1,0:T(8,128)(2,1)} %param.16) | copy-start | bytes 1572868
  7.2 60.8 %all-gather.3.cloned.1.call-start = ((), (), s32[]{:S(2)}) async-start(), calls=%async_computation | async-start | bytes 3096576 | tf_op jit(solution)/shard_map/all_gather | solution.py:48
  9.1 98.9 %copy-start.5 = (bf16[1,128,2048]{2,1,0:T(8,128)(2,1)S(1)}, bf16[1,128,2048]{2,1,0:T(8,128)(2,1)}, u32[]{:S(2)}) copy-start(bf16[1,128,2048]{2,1,0:T(8,128)(2,1)} %param.11) | copy-start | bytes 1572868
  9.1 122.3 %all-gather.5.cloned.1.call-start = ((), (), s32[]{:S(2)}) async-start(), calls=%async_computation.1 | async-start | bytes 8257536 | tf_op jit(solution)/shard_map/all_gather | solution.py:49
  68.0 40.5 %copy-start.7 = (bf16[2688,16]{0,1:T(8,128)(2,1)S(1)}, bf16[2688,16]{0,1:T(8,128)(2,1)}, u32[]{:S(2)}) copy-start(bf16[2688,16]{0,1:T(8,128)(2,1)} %param.14) | copy-start | bytes 258052
  68.1 283.8 %all-reduce.4.cloned.1.call-start = ((), (), s32[]{:S(2)}) async-start(), calls=%async_computation.2 | async-start | bytes 475136 | tf_op jit(solution)/shard_map/psum | solution.py:143
  68.1 44.5 %collective-permute-start = (bf16[128,1024]{1,0:T(8,128)(2,1)}, bf16[128,1024]{1,0:T(8,128)(2,1)S(1)}, u32[]{:S(2)}, u32[]{:S(2)}) collective-permute-start(bf16[128,1024]{1,0:T(8,128)(2,1)} %bitcast.3), channel_id=1, source_target_pairs={{0,14},{1,15},{16,30},{17,31}} | collective-permute-start | bytes 786440 | tf_op jit(solution)/shard_map/ppermute | solution.py:23
  68.8 48.7 %collective-permute-start.1 = (bf16[128,1024]{1,0:T(8,128)(2,1)}, bf16[128,1024]{1,0:T(8,128)(2,1)}, u32[]{:S(2)}, u32[]{:S(2)}) collective-permute-start(bf16[128,1024]{1,0:T(8,128)(2,1)} %bitcast.3), channel_id=1, source_target_pairs={{0,12},{2,14},{1,13},{3,15},{16,28},{18,30},{17,29},{19,31}} | collective-permute-start | bytes 786440 | tf_op jit(solution)/shard_map/ppermute | solution.py:23
  70.2 50.3 %collective-permute-start.2 = (bf16[128,1024]{1,0:T(8,128)(2,1)}, bf16[128,1024]{1,0:T(8,128)(2,1)}, u32[]{:S(2)}, u32[]{:S(2)}) collective-permute-start(bf16[128,1024]{1,0:T(8,128)(2,1)} %bitcast.3), channel_id=1, source_target_pairs={{0,10},{2,12},{4,14},{1,11},{3,13},{5,15},{16,26},{18,28},{20,30},... | collective-permute-start | bytes 786440 | tf_op jit(solution)/shard_map/ppermute | solution.py:23
  74.3 47.1 %collective-permute-start.3 = (bf16[128,1024]{1,0:T(8,128)(2,1)}, bf16[128,1024]{1,0:T(8,128)(2,1)}, u32[]{:S(2)}, u32[]{:S(2)}) collective-permute-start(bf16[128,1024]{1,0:T(8,128)(2,1)} %bitcast.3), channel_id=1, source_target_pairs={{0,8},{2,10},{4,12},{6,14},{1,9},{3,11},{5,13},{7,15},{16,24},{18,... | collective-permute-start | bytes 786440 | tf_op jit(solution)/shard_map/ppermute | solution.py:23
  106.8 2.0 collective-permute-start.7
  108.8 13.6 %collective-permute-start.4 = (bf16[128,1024]{1,0:T(8,128)(2,1)}, bf16[128,1024]{1,0:T(8,128)(2,1)S(1)}, u32[]{:S(2)}, u32[]{:S(2)}) collective-permute-start(bf16[128,1024]{1,0:T(8,128)(2,1)} %bitcast.3), channel_id=1, source_target_pairs={{0,6},{2,8},{4,10},{6,12},{8,14},{1,7},{3,9},{5,11},{7,13},{9,15},... | collective-permute-start | bytes 786440 | tf_op jit(solution)/shard_map/ppermute | solution.py:23
  112.6 0.7 copy-start.8
  113.4 12.9 %collective-permute-start.5 = (bf16[128,1024]{1,0:T(8,128)(2,1)}, bf16[128,1024]{1,0:T(8,128)(2,1)S(1)}, u32[]{:S(2)}, u32[]{:S(2)}) collective-permute-start(bf16[128,1024]{1,0:T(8,128)(2,1)} %bitcast.3), channel_id=1, source_target_pairs={{0,4},{2,6},{4,8},{6,10},{8,12},{10,14},{1,5},{3,7},{5,9},{7,11},{... | collective-permute-start | bytes 786440 | tf_op jit(solution)/shard_map/ppermute | solution.py:23
  117.5 12.9 %collective-permute-start.6 = (bf16[128,1024]{1,0:T(8,128)(2,1)}, bf16[128,1024]{1,0:T(8,128)(2,1)S(1)}, u32[]{:S(2)}, u32[]{:S(2)}) collective-permute-start(bf16[128,1024]{1,0:T(8,128)(2,1)} %bitcast.3), channel_id=1, source_target_pairs={{0,2},{2,4},{4,6},{6,8},{8,10},{10,12},{12,14},{1,3},{3,5},{5,7},{... | collective-permute-start | bytes 786440 | tf_op jit(solution)/shard_map/ppermute | solution.py:23
  131.4 4.2 %copy-start.9 = (bf16[16,1024]{1,0:T(8,128)(2,1)S(1)}, bf16[16,1024]{1,0:T(8,128)(2,1)}, u32[]{:S(2)}) copy-start(bf16[16,1024]{1,0:T(8,128)(2,1)} %param.15) | copy-start | bytes 98308
  136.7 31.4 %collective-permute-start.15 = (bf16[128,1024]{0,1:T(8,128)(2,1)}, bf16[128,1024]{0,1:T(8,128)(2,1)}, u32[]{:S(2)}, u32[]{:S(2)}) collective-permute-start(bf16[128,1024]{0,1:T(8,128)(2,1)} %fusion.15), channel_id=1, source_target_pairs={{0,14},{1,15},{16,30},{17,31}} | collective-permute-start | bytes 786440 | tf_op jit(solution)/shard_map/ppermute | solution.py:23
  138.0 34.0 %collective-permute-start.16 = (bf16[128,1024]{0,1:T(8,128)(2,1)}, bf16[128,1024]{0,1:T(8,128)(2,1)}, u32[]{:S(2)}, u32[]{:S(2)}) collective-permute-start(bf16[128,1024]{0,1:T(8,128)(2,1)} %fusion.15), channel_id=1, source_target_pairs={{0,12},{2,14},{1,13},{3,15},{16,28},{18,30},{17,29},{19,31}} | collective-permute-start | bytes 786440 | tf_op jit(solution)/shard_map/ppermute | solution.py:23
  139.4 35.6 %collective-permute-start.17 = (bf16[128,1024]{0,1:T(8,128)(2,1)}, bf16[128,1024]{0,1:T(8,128)(2,1)}, u32[]{:S(2)}, u32[]{:S(2)}) collective-permute-start(bf16[128,1024]{0,1:T(8,128)(2,1)} %fusion.15), channel_id=1, source_target_pairs={{0,10},{2,12},{4,14},{1,11},{3,13},{5,15},{16,26},{18,28},{20,30},... | collective-permute-start | bytes 786440 | tf_op jit(solution)/shard_map/ppermute | solution.py:23
  141.6 35.1 %collective-permute-start.18 = (bf16[128,1024]{0,1:T(8,128)(2,1)}, bf16[128,1024]{0,1:T(8,128)(2,1)}, u32[]{:S(2)}, u32[]{:S(2)}) collective-permute-start(bf16[128,1024]{0,1:T(8,128)(2,1)} %fusion.15), channel_id=1, source_target_pairs={{0,8},{2,10},{4,12},{6,14},{1,9},{3,11},{5,13},{7,15},{16,24},{18,... | collective-permute-start | bytes 786440 | tf_op jit(solution)/shard_map/ppermute | solution.py:23
  148.2 30.3 %collective-permute-start.19 = (bf16[128,1024]{0,1:T(8,128)(2,1)}, bf16[128,1024]{0,1:T(8,128)(2,1)}, u32[]{:S(2)}, u32[]{:S(2)}) collective-permute-start(bf16[128,1024]{0,1:T(8,128)(2,1)} %fusion.15), channel_id=1, source_target_pairs={{0,6},{2,8},{4,10},{6,12},{8,14},{1,7},{3,9},{5,11},{7,13},{9,15},... | collective-permute-start | bytes 786440 | tf_op jit(solution)/shard_map/ppermute | solution.py:23
  162.3 25.8 %slice-start = ((s8[8388608]{0:T(1024)(128)(4,1)}), s8[4194304]{0:T(1024)(128)(4,1)S(1)}, s32[]{:S(2)}) async-start(s8[8388608]{0:T(1024)(128)(4,1)} %bitcast.121), calls=%async_computation.3 | async-start | bytes 8388608
  162.3 25.8 %slice-start.1 = ((s8[8388608]{0:T(1024)(128)(4,1)}), s8[4194304]{0:T(1024)(128)(4,1)S(1)}, s32[]{:S(2)}) async-start(s8[8388608]{0:T(1024)(128)(4,1)} %bitcast.121), calls=%async_computation.4 | async-start | bytes 8388608
  168.0 20.1 %copy-start.6 = (bf16[128,8,2,128]{3,2,1,0:T(2,128)(2,1)S(1)}, bf16[128,8,2,128]{3,2,1,0:T(2,128)(2,1)}, u32[]{:S(2)}) copy-start(bf16[128,8,2,128]{3,2,1,0:T(2,128)(2,1)} %reshape_squeeze.7) | copy-start | bytes 1572868
  168.0 15.9 %collective-permute-start.20 = (bf16[128,1024]{0,1:T(8,128)(2,1)}, bf16[128,1024]{0,1:T(8,128)(2,1)S(1)}, u32[]{:S(2)}, u32[]{:S(2)}) collective-permute-start(bf16[128,1024]{0,1:T(8,128)(2,1)} %fusion.15), channel_id=1, source_target_pairs={{0,4},{2,6},{4,8},{6,10},{8,12},{10,14},{1,5},{3,7},{5,9},{7,11},{... | collective-permute-start | bytes 786440 | tf_op jit(solution)/shard_map/ppermute | solution.py:23
  172.0 13.5 %collective-permute-start.21 = (bf16[128,1024]{0,1:T(8,128)(2,1)}, bf16[128,1024]{0,1:T(8,128)(2,1)S(1)}, u32[]{:S(2)}, u32[]{:S(2)}) collective-permute-start(bf16[128,1024]{0,1:T(8,128)(2,1)} %fusion.15), channel_id=1, source_target_pairs={{0,2},{2,4},{4,6},{6,8},{8,10},{10,12},{12,14},{1,3},{3,5},{5,7},{... | collective-permute-start | bytes 786440 | tf_op jit(solution)/shard_map/ppermute | solution.py:23
  175.0 18.5 %collective-permute-start.14 = (bf16[128,1024]{0,1:T(8,128)(2,1)S(1)}, bf16[128,1024]{0,1:T(8,128)(2,1)S(1)}, u32[]{:S(2)}, u32[]{:S(2)}) collective-permute-start(bf16[128,1024]{0,1:T(8,128)(2,1)S(1)} %bitcast.141), channel_id=1, source_target_pairs={{14,0},{15,1},{30,16},{31,17}} | collective-permute-start | bytes 786440 | tf_op jit(solution)/shard_map/ppermute | solution.py:23
  176.7 19.6 %collective-permute-start.13 = (bf16[128,1024]{0,1:T(8,128)(2,1)S(1)}, bf16[128,1024]{0,1:T(8,128)(2,1)S(1)}, u32[]{:S(2)}, u32[]{:S(2)}) collective-permute-start(bf16[128,1024]{0,1:T(8,128)(2,1)S(1)} %bitcast.140), channel_id=1, source_target_pairs={{12,0},{14,2},{13,1},{15,3},{28,16},{30,18},{29,17},{31,19}} | collective-permute-start | bytes 786440 | tf_op jit(solution)/shard_map/ppermute | solution.py:23
  178.4 24.5 %collective-permute-start.12 = (bf16[128,1024]{0,1:T(8,128)(2,1)S(1)}, bf16[128,1024]{0,1:T(8,128)(2,1)S(1)}, u32[]{:S(2)}, u32[]{:S(2)}) collective-permute-start(bf16[128,1024]{0,1:T(8,128)(2,1)S(1)} %bitcast.139), channel_id=1, source_target_pairs={{10,0},{12,2},{14,4},{11,1},{13,3},{15,5},{26,16},{28,18},{30,20},... | collective-permute-start | bytes 786440 | tf_op jit(solution)/shard_map/ppermute | solution.py:23
  184.0 19.2 %collective-permute-start.11 = (bf16[128,1024]{0,1:T(8,128)(2,1)S(1)}, bf16[128,1024]{0,1:T(8,128)(2,1)S(1)}, u32[]{:S(2)}, u32[]{:S(2)}) collective-permute-start(bf16[128,1024]{0,1:T(8,128)(2,1)S(1)} %bitcast.138), channel_id=1, source_target_pairs={{8,0},{10,2},{12,4},{14,6},{9,1},{11,3},{13,5},{15,7},{24,16},{26,... | collective-permute-start | bytes 786440 | tf_op jit(solution)/shard_map/ppermute | solution.py:23
  185.5 37.2 %collective-permute-start.10 = (bf16[128,1024]{0,1:T(8,128)(2,1)S(1)}, bf16[128,1024]{0,1:T(8,128)(2,1)S(1)}, u32[]{:S(2)}, u32[]{:S(2)}) collective-permute-start(bf16[128,1024]{0,1:T(8,128)(2,1)S(1)} %bitcast.137), channel_id=1, source_target_pairs={{6,0},{8,2},{10,4},{12,6},{14,8},{7,1},{9,3},{11,5},{13,7},{15,9},... | collective-permute-start | bytes 786440 | tf_op jit(solution)/shard_map/ppermute | solution.py:23
  193.4 30.7 %collective-permute-start.9 = (bf16[128,1024]{0,1:T(8,128)(2,1)S(1)}, bf16[128,1024]{0,1:T(8,128)(2,1)S(1)}, u32[]{:S(2)}, u32[]{:S(2)}) collective-permute-start(bf16[128,1024]{0,1:T(8,128)(2,1)S(1)} %bitcast.136), channel_id=1, source_target_pairs={{4,0},{6,2},{8,4},{10,6},{12,8},{14,10},{5,1},{7,3},{9,5},{11,7},{... | collective-permute-start | bytes 786440 | tf_op jit(solution)/shard_map/ppermute | solution.py:23
  196.3 27.8 %collective-permute-start.8 = (bf16[128,1024]{0,1:T(8,128)(2,1)S(1)}, bf16[128,1024]{0,1:T(8,128)(2,1)S(1)}, u32[]{:S(2)}, u32[]{:S(2)}) collective-permute-start(bf16[128,1024]{0,1:T(8,128)(2,1)S(1)} %bitcast.135), channel_id=1, source_target_pairs={{2,0},{4,2},{6,4},{8,6},{10,8},{12,10},{14,12},{3,1},{5,3},{7,5},{... | collective-permute-start | bytes 786440 | tf_op jit(solution)/shard_map/ppermute | solution.py:23
  228.8 9.0 %copy-start.3 = (bf16[128,8,128]{0,2,1:T(8,128)(2,1)S(1)}, bf16[128,8,128]{0,2,1:T(8,128)(2,1)}, u32[]{:S(2)}) copy-start(bf16[128,8,128]{0,2,1:T(8,128)(2,1)} %get-tuple-element.31) | copy-start | bytes 786436
  228.8 11.1 %copy-start.2 = (bf16[128,8,128]{0,2,1:T(8,128)(2,1)S(1)}, bf16[128,8,128]{0,2,1:T(8,128)(2,1)}, u32[]{:S(2)}) copy-start(bf16[128,8,128]{0,2,1:T(8,128)(2,1)} %get-tuple-element.32) | copy-start | bytes 786436
  228.8 13.3 %copy-start.1 = (bf16[128,8,128]{0,2,1:T(8,128)(2,1)S(1)}, bf16[128,8,128]{0,2,1:T(8,128)(2,1)}, u32[]{:S(2)}) copy-start(bf16[128,8,128]{0,2,1:T(8,128)(2,1)} %get-tuple-element.33) | copy-start | bytes 786436
  230.7 14.8 %collective-permute-start.28 = (bf16[128,1024]{1,0:T(8,128)(2,1)}, bf16[128,1024]{1,0:T(8,128)(2,1)S(1)}, u32[]{:S(2)}, u32[]{:S(2)}) collective-permute-start(bf16[128,1024]{1,0:T(8,128)(2,1)} %copy.53), channel_id=1, source_target_pairs={{14,0},{15,1},{30,16},{31,17}} | collective-permute-start | bytes 786440 | tf_op jit(solution)/shard_map/ppermute | solution.py:23
  233.2 14.2 %collective-permute-start.27 = (bf16[128,1024]{1,0:T(8,128)(2,1)}, bf16[128,1024]{1,0:T(8,128)(2,1)S(1)}, u32[]{:S(2)}, u32[]{:S(2)}) collective-permute-start(bf16[128,1024]{1,0:T(8,128)(2,1)} %copy.52), channel_id=1, source_target_pairs={{12,0},{14,2},{13,1},{15,3},{28,16},{30,18},{29,17},{31,19}} | collective-permute-start | bytes 786440 | tf_op jit(solution)/shard_map/ppermute | solution.py:23
  235.7 19.1 %collective-permute-start.26 = (bf16[128,1024]{1,0:T(8,128)(2,1)}, bf16[128,1024]{1,0:T(8,128)(2,1)S(1)}, u32[]{:S(2)}, u32[]{:S(2)}) collective-permute-start(bf16[128,1024]{1,0:T(8,128)(2,1)} %copy.51), channel_id=1, source_target_pairs={{10,0},{12,2},{14,4},{11,1},{13,3},{15,5},{26,16},{28,18},{30,20},... | collective-permute-start | bytes 786440 | tf_op jit(solution)/shard_map/ppermute | solution.py:23
  238.7 16.0 %collective-permute-start.25 = (bf16[128,1024]{1,0:T(8,128)(2,1)}, bf16[128,1024]{1,0:T(8,128)(2,1)S(1)}, u32[]{:S(2)}, u32[]{:S(2)}) collective-permute-start(bf16[128,1024]{1,0:T(8,128)(2,1)} %copy.50), channel_id=1, source_target_pairs={{8,0},{10,2},{12,4},{14,6},{9,1},{11,3},{13,5},{15,7},{24,16},{26,... | collective-permute-start | bytes 786440 | tf_op jit(solution)/shard_map/ppermute | solution.py:23
  240.8 30.2 %collective-permute-start.24 = (bf16[128,1024]{1,0:T(8,128)(2,1)}, bf16[128,1024]{1,0:T(8,128)(2,1)}, u32[]{:S(2)}, u32[]{:S(2)}) collective-permute-start(bf16[128,1024]{1,0:T(8,128)(2,1)} %copy.49), channel_id=1, source_target_pairs={{6,0},{8,2},{10,4},{12,6},{14,8},{7,1},{9,3},{11,5},{13,7},{15,9},... | collective-permute-start | bytes 786440 | tf_op jit(solution)/shard_map/ppermute | solution.py:23
  245.5 29.5 %collective-permute-start.23 = (bf16[128,1024]{1,0:T(8,128)(2,1)}, bf16[128,1024]{1,0:T(8,128)(2,1)S(1)}, u32[]{:S(2)}, u32[]{:S(2)}) collective-permute-start(bf16[128,1024]{1,0:T(8,128)(2,1)} %copy.48), channel_id=1, source_target_pairs={{4,0},{6,2},{8,4},{10,6},{12,8},{14,10},{5,1},{7,3},{9,5},{11,7},{... | collective-permute-start | bytes 786440 | tf_op jit(solution)/shard_map/ppermute | solution.py:23
  247.4 27.6 %collective-permute-start.22 = (bf16[128,1024]{1,0:T(8,128)(2,1)}, bf16[128,1024]{1,0:T(8,128)(2,1)S(1)}, u32[]{:S(2)}, u32[]{:S(2)}) collective-permute-start(bf16[128,1024]{1,0:T(8,128)(2,1)} %copy.46), channel_id=1, source_target_pairs={{2,0},{4,2},{6,4},{8,6},{10,8},{12,10},{14,12},{3,1},{5,3},{7,5},{... | collective-permute-start | bytes 786440 | tf_op jit(solution)/shard_map/ppermute | solution.py:23
Sparse Core Ops, SparseCore 0:
  10.8 57.1 all-gather.2
  69.6 14.4 all-gather.4
  245.2 106.5 all-reduce.3
where the time goes:
time: 363 us; the launch traced here: 361 us
  waiting for transfers between devices  187 us (52%)
  starting transfers between devices  55.1 us (15%)
  local copies, waits for them, and re-layouts  37.7 us (10%)
  matrix products  32 us (9%)
  blocking collectives  30.3 us (8%)
  between operations  14.4 us (4%)
  other arithmetic  5.29 us (1%)
    psum x1, waiting for transfers between devices, shards(): lax.psum((down_factor, up_factor), ('ctx', 'pair'))  74.8 us
    all_gather x1, waiting for transfers between devices, shards(): rows_half = lax.all_gather(own_half, 'ctx', axis=0, tiled=True)  58.9 us
    ppermute x28, starting transfers between devices, shifted(): return lax.ppermute(block, axis, route)  55 us
    ppermute x28, waiting for transfers between devices, shifted(): return lax.ppermute(block, axis, route)  52.8 us
    psum x1, blocking collectives, shards(): own_diff, counts = lax.psum((part_diff, part_count), 'ctx')  30.3 us
    unnamed x48, local copies, waits for them, and re-layouts  17.1 us
    convert_element_type x7, local copies, waits for them, and re-layouts, shards(): key_parts[block_start:block_start + tok_rows].astype(jnp.bfloat16)  8.84 us
  transfers between devices with their start and end apart: 32, of which 11 were waited for; matrix products, arithmetic and copies ran while one was open for 16% of the time, Pallas kernels for 0%

commit v1 on v0

--- a/solution.py
+++ b/solution.py
@@ -11,6 +11,12 @@
 ADAPTER_SCALE = 2.0
 ATTN_SCALE = 168.0 ** (-0.5)
 NEG_FILL = -1e30
+
+
+def begin_the_racks(my_data, dimension_no):
+    mixed_arr = list(my_data.shape[1:])
+    mixed_arr[dimension_no] *= my_data.shape[0]
+    return jnp.moveaxis(my_data, 0, dimension_no).reshape(mixed_arr)
 
 
 def from_partner(shard, axis, stride):
@@ -45,7 +51,23 @@
     ctx_index = lax.axis_index("ctx")
     half_cols = width_kv // 2
     own_half = lax.dynamic_slice_in_dim(value_projection, pair_index * half_cols, half_cols, 1)
-    rows_half = lax.all_gather(own_half, "ctx", axis=0, tiled=True)
+    n_shards = lax.axis_size("ctx")
+    table = []
+    for to_i in range(n_shards):
+        table.append((to_i, (to_i + 1) % n_shards))
+    so_far_all = []
+    for dev_i, idx in table:
+        so_far_all.append((idx, dev_i))
+    taken_in, w_next = ([], [])
+    for c in range(n_shards - 1):
+        if c % 2 == 0:
+            taken_in.append(lax.ppermute(taken_in[-1] if taken_in else own_half, "ctx", table))
+        else:
+            w_next.append(lax.ppermute(w_next[-1] if w_next else own_half, "ctx", so_far_all))
+    passed = jnp.stack([*taken_in[::-1], own_half, *w_next], axis=0)
+    p_next = lax.axis_index("ctx") - len(taken_in)
+    passed = passed[(jnp.arange(n_shards) - p_next) % n_shards]
+    rows_half = begin_the_racks(passed, 0)
     full_weight = lax.all_gather(rows_half, "pair", axis=1, tiled=True)
     rank_projection = jnp.dot(hidden_rows, adapter_down, preferred_element_type=jnp.float32).astype(
         jnp.bfloat16

time: 363 us -> 370 us (1.019)
  waiting for transfers between devices: 187 us -> 170 us
  starting transfers between devices: 55.1 us -> 71.9 us
  local copies, waits for them, and re-layouts: 37.7 us -> 46.1 us
    all_gather x1 -> x0, waiting for transfers between devices: 58.9 us -> none  [shards(): rows_half = lax.all_gather(own_half, 'ctx', axis=0, tiled=True)]
    ppermute x0 -> x7, waiting for transfers between devices: none -> 43.4 us  [the longest x4 33.7 us: shards(): lax.ppermute(taken_in[-1] if taken_in else own_half, 'ctx', table)]
    ppermute x0 -> x7, starting transfers between devices: none -> 10.9 us  [the longest x3 6.27 us: shards(): lax.ppermute(w_next[-1] if w_next else own_half, 'ctx', so_far_all)]
    ppermute x28, starting transfers between devices: 55 us -> 60.9 us  [shifted(): return lax.ppermute(block, axis, route)]
    unnamed x48 -> x65, local copies, waits for them, and re-layouts: 17.1 us -> 23 us
  transfers between devices with their start and end apart: 32 -> 38, of which waited for: 11 -> 17; matrix products, arithmetic and copies ran while one was open for 16% -> 17% of each run, Pallas kernels for 0% -> 0%
where the time goes in v1:
time: 370 us; the launch traced here: 369 us
  waiting for transfers between devices  170 us (46%)
  starting transfers between devices  71.9 us (19%)
  local copies, waits for them, and re-layouts  46.1 us (12%)
  matrix products  32 us (9%)
  blocking collectives  28.7 us (8%)
  between operations  14.7 us (4%)
  other arithmetic  5.32 us (1%)
    psum x1, waiting for transfers between devices, shards(): lax.psum((down_factor, up_factor), ('ctx', 'pair'))  73.5 us
    ppermute x28, starting transfers between devices, shifted(): return lax.ppermute(block, axis, route)  60.9 us
    ppermute x28, waiting for transfers between devices, shifted(): return lax.ppermute(block, axis, route)  52.9 us
    ppermute x4, waiting for transfers between devices, shards(): lax.ppermute(taken_in[-1] if taken_in else own_half, 'ctx', table)  33.7 us
    psum x1, blocking collectives, shards(): own_diff, counts = lax.psum((part_diff, part_count), 'ctx')  28.7 us
    unnamed x65, local copies, waits for them, and re-layouts  23 us
    convert_element_type x7, local copies, waits for them, and re-layouts, shards(): key_parts[block_start:block_start + tok_rows].astype(jnp.bfloat16)  9.84 us
    ppermute x3, waiting for transfers between devices, shards(): lax.ppermute(w_next[-1] if w_next else own_half, 'ctx', so_far_all)  9.64 us
  transfers between devices with their start and end apart: 38, of which 17 were waited for; matrix products, arithmetic and copies ran while one was open for 17% of the time, Pallas kernels for 0%

profile of v1, /device:TPU:8, one launch (start us, length us, event | category | flops | bytes accessed | tf_op | source)
XLA Modules:
  0.0 368.7 jit_solution(17221334742173083109)
XLA Ops:
  9.8 9.2 %collective-permute-done.7 = bf16[336,512]{1,0:T(8,128)(2,1)S(1)} collective-permute-done((bf16[336,512]{1,0:T(8,128)(2,1)S(1)}, bf16[336,512]{1,0:T(8,128)(2,1)S(1)}, u32[]{:S(2)}, u32[]{:S(2)}) %collective-permute-start.7) | collective-permute-done | bytes 344096 | tf_op jit(solution)/shard_map/ppermute | solution.py:64
  20.4 2.3 collective-permute-start.11
  22.7 11.5 %collective-permute-done.8 = bf16[336,512]{1,0:T(8,128)(2,1)S(1)} collective-permute-done((bf16[336,512]{1,0:T(8,128)(2,1)S(1)}, bf16[336,512]{1,0:T(8,128)(2,1)S(1)}, u32[]{:S(2)}, u32[]{:S(2)}) %collective-permute-start.8) | collective-permute-done | bytes 344096 | tf_op jit(solution)/shard_map/ppermute | solution.py:64
  34.2 2.5 collective-permute-start.9
  37.0 2.2 collective-permute-start.12
  39.2 6.4 %collective-permute-done.9 = bf16[336,512]{1,0:T(8,128)(2,1)S(1)} collective-permute-done((bf16[336,512]{1,0:T(8,128)(2,1)S(1)}, bf16[336,512]{1,0:T(8,128)(2,1)S(1)}, u32[]{:S(2)}, u32[]{:S(2)}) %collective-permute-start.9) | collective-permute-done | bytes 344096 | tf_op jit(solution)/shard_map/ppermute | solution.py:64
  45.6 7.3 %collective-permute-done.12 = bf16[336,512]{1,0:T(8,128)(2,1)} collective-permute-done((bf16[336,512]{1,0:T(8,128)(2,1)S(1)}, bf16[336,512]{1,0:T(8,128)(2,1)}, u32[]{:S(2)}, u32[]{:S(2)}) %collective-permute-start.12) | collective-permute-done | bytes 344096 | tf_op jit(solution)/shard_map/ppermute | solution.py:66
  52.9 1.7 collective-permute-start.13
  54.7 6.7 %collective-permute-done.10 = bf16[336,512]{1,0:T(8,128)(2,1)} collective-permute-done((bf16[336,512]{1,0:T(8,128)(2,1)S(1)}, bf16[336,512]{1,0:T(8,128)(2,1)}, u32[]{:S(2)}, u32[]{:S(2)}) %collective-permute-start.10) | collective-permute-done | bytes 344096 | tf_op jit(solution)/shard_map/ppermute | solution.py:64
  66.5 2.0 collective-permute-done.13
  68.5 2.3 gather_fusion
  73.1 10.0 %collective-permute-start.2 = (bf16[128,1024]{1,0:T(8,128)(2,1)}, bf16[128,1024]{1,0:T(8,128)(2,1)}, u32[]{:S(2)}, u32[]{:S(2)}) collective-permute-start(bf16[128,1024]{1,0:T(8,128)(2,1)} %bitcast.3), channel_id=1, source_target_pairs={{0,10},{2,12},{4,14},{1,11},{3,13},{5,15},{16,26},{18,28},{20,30},... | collective-permute-start | bytes 786440 | tf_op jit(solution)/shard_map/ppermute | solution.py:29
  83.1 2.0 collective-permute-start.3
  85.2 28.7 %all-reduce.1 = (f32[8]{0:T(128)S(1)}, f32[8]{0:T(128)S(1)}) all-reduce(f32[8]{0:T(128)S(1)} %get-tuple-element.21, f32[8]{0:T(128)S(1)} %get-tuple-element.22), channel_id=1, replica_groups=mesh['grp'=2,'ctx'=8,'pair'=2] {'ctx'}, use_global_device_ids=true, to_apply=%region_1.2 | all-reduce | flops 16 | bytes 128 | tf_op jit(solution)/shard_map/psum | solution.py:86
  115.9 2.9 collective-permute-start.4
  120.5 3.2 collective-permute-start.5
  124.7 1.9 collective-permute-start.6
  129.6 3.8 %collective-permute-done.5 = bf16[128,1024]{1,0:T(8,128)(2,1)S(1)} collective-permute-done((bf16[128,1024]{1,0:T(8,128)(2,1)}, bf16[128,1024]{1,0:T(8,128)(2,1)S(1)}, u32[]{:S(2)}, u32[]{:S(2)}) %collective-permute-start.5) | collective-permute-done | bytes 262176 | tf_op jit(solution)/shard_map/ppermute | solution.py:29
  133.4 4.2 %collective-permute-done.6 = bf16[128,1024]{1,0:T(8,128)(2,1)S(1)} collective-permute-done((bf16[128,1024]{1,0:T(8,128)(2,1)}, bf16[128,1024]{1,0:T(8,128)(2,1)S(1)}, u32[]{:S(2)}, u32[]{:S(2)}) %collective-permute-start.6) | collective-permute-done | bytes 262176 | tf_op jit(solution)/shard_map/ppermute | solution.py:29
  138.6 4.2 %convolution_bitcast_fusion.1 = f32[128,1024]{0,1:T(8,128)S(1)} fusion(bf16[2688,1024]{1,0:T(8,128)(2,1)} %all-gather.2.cloned.1.call-done, bf16[1,128,2688]{2,1,0:T(8,128)(2,1)S(1)} %copy-done), kind=kOutput, calls=%fused_computation.27 | convolution fusion | flops 704643072 | bytes 6717440 | tf_op jit(solution)/shard_map/dot_general | solution.py:76
  146.5 2.3 collective-permute-start.24
  148.8 6.5 %collective-permute-start.25 = (bf16[128,1024]{0,1:T(8,128)(2,1)}, bf16[128,1024]{0,1:T(8,128)(2,1)}, u32[]{:S(2)}, u32[]{:S(2)}) collective-permute-start(bf16[128,1024]{0,1:T(8,128)(2,1)} %fusion.15), channel_id=1, source_target_pairs={{0,8},{2,10},{4,12},{6,14},{1,9},{3,11},{5,13},{7,15},{16,24},{18,... | collective-permute-start | bytes 786440 | tf_op jit(solution)/shard_map/ppermute | solution.py:29
  155.3 2.0 collective-permute-start.26
  157.3 2.0 copy.71
  159.3 3.2 copy.60
  162.5 6.9 %fusion.38 = (f32[8,2,128]{2,1,0:T(2,128)S(1)}, f32[8,2,128,1024]{2,3,1,0:T(8,128)}) fusion(pred[128,1024]{0,1:T(8,128)(4,1)} %compare_and_fusion, bf16[1024,8,128,1]{0,2,3,1:T(8,128)(2,1)S(1)} %copy.60, bf16[128,8,2,128]{0,3,2,1:T(8,128)(2,1)S(1)} %bitcast.146), kind=kOutput, calls=%fused_computation.98 | convolution fusion | flops 547357696 | bytes 11149312 | tf_op jit(solution)/shard_map/sub | solution.py:121
  169.4 5.1 %fusion.39 = (bf16[1024,8,128]{0,2,1:T(8,128)(2,1)S(1)}, f32[1024,8,128]{0,2,1:T(8,128)S(1)}) fusion(bf16[128,8,2,128]{3,2,1,0:T(2,128)(2,1)} %reshape_squeeze.7, f32[128]{0:T(128)S(1)} %get-tuple-element.20, f32[8,2,128,1024]{2,3,1,0:T(8,128)} %get-tuple-element.42, f32[8,2,128]{2,1,0:T(2,128)S(1)} %get-tuple-element.41), kind=kOutput, calls=%fused_computation.99 | convolution fusion | flops 544210944 | bytes 15213056 | tf_op jit(solution)/shard_map/jgtl,tjgd->ljd/dot_general | solution.py:137
  175.2 2.9 collective-permute-start.27
  179.1 1.9 collective-permute-start.28
  187.9 3.2 collective-permute-done.27
  195.3 1.9 fusion.1
  197.2 1.7 fusion.3
  200.6 2.9 collective-permute-start.16
  203.5 3.1 collective-permute-start.15
  206.6 3.4 fusion.40
  210.3 19.5 %collective-permute-done.17 = bf16[128,1024]{0,1:T(8,128)(2,1)S(1)} collective-permute-done((bf16[128,1024]{0,1:T(8,128)(2,1)S(1)}, bf16[128,1024]{0,1:T(8,128)(2,1)S(1)}, u32[]{:S(2)}, u32[]{:S(2)}) %collective-permute-start.17) | collective-permute-done | bytes 262176 | tf_op jit(solution)/shard_map/ppermute | solution.py:29
  232.5 2.0 copy.54
  236.0 1.9 copy.53
  238.5 1.8 copy.52
  241.0 1.8 copy.51
  245.0 1.8 copy.50
  253.7 1.9 collective-permute-start.30
  255.6 1.9 collective-permute-start.29
  257.5 5.3 %fusion.11 = bf16[1,128,2688]{2,1,0:T(8,128)(2,1)} fusion(f32[128,2688]{1,0:T(8,128)S(1)} %convolution_multiply_fusion, bf16[128,1024]{0,1:T(8,128)(2,1)S(1)} %fusion.27, bf16[2688,1024]{1,0:T(8,128)(2,1)} %all-gather.2.cloned.1.call-done), kind=kOutput, calls=%fused_computation.20 | convolution fusion | flops 705331200 | bytes 7831552 | tf_op jit(solution)/shard_map/tk,dk->td/dot_general | solution.py:155
  262.9 15.2 %collective-permute-done.31 = bf16[128,1024]{1,0:T(8,128)(2,1)} collective-permute-done((bf16[128,1024]{1,0:T(8,128)(2,1)}, bf16[128,1024]{1,0:T(8,128)(2,1)}, u32[]{:S(2)}, u32[]{:S(2)}) %collective-permute-start.31) | collective-permute-done | bytes 262176 | tf_op jit(solution)/shard_map/ppermute | solution.py:29
  278.1 5.2 %collective-permute-done.30 = bf16[128,1024]{1,0:T(8,128)(2,1)S(1)} collective-permute-done((bf16[128,1024]{1,0:T(8,128)(2,1)}, bf16[128,1024]{1,0:T(8,128)(2,1)S(1)}, u32[]{:S(2)}, u32[]{:S(2)}) %collective-permute-start.30) | collective-permute-done | bytes 262176 | tf_op jit(solution)/shard_map/ppermute | solution.py:29
  283.3 2.0 fusion.31
  285.3 73.5 %all-reduce.4.cloned.1.call-done = (f32[2688,16]{0,1:T(8,128)}, f32[16,1024]{1,0:T(8,128)}) async-done(((f32[2688,16]{0,1:T(8,128)}, f32[16,1024]{1,0:T(8,128)}), (f32[2688,16]{0,1:T(8,128)}, f32[16,1024]{1,0:T(8,128)})) %all-reduce.4.cloned.1.call-update) | async-done | bytes 237584 | tf_op jit(solution)/shard_map/psum | solution.py:165
  (145 shorter events, 56.0 us)
Async XLA Ops:
  7.2 108.5 %copy-start = (bf16[1,128,2688]{2,1,0:T(8,128)(2,1)S(1)}, bf16[1,128,2688]{2,1,0:T(8,128)(2,1)}, u32[]{:S(2)}) copy-start(bf16[1,128,2688]{2,1,0:T(8,128)(2,1)} %param.10) | copy-start | bytes 2064388
  7.2 131.4 %all-gather.2.cloned.1.call-start = ((), (), s32[]{:S(2)}) async-start(), calls=%async_computation | async-start | bytes 8257536 | tf_op jit(solution)/shard_map/all_gather | solution.py:71
  8.3 10.8 %collective-permute-start.7 = (bf16[336,512]{1,0:T(8,128)(2,1)S(1)}, bf16[336,512]{1,0:T(8,128)(2,1)S(1)}, u32[]{:S(2)}, u32[]{:S(2)}) collective-permute-start(bf16[336,512]{1,0:T(8,128)(2,1)S(1)} %constant_dynamic-slice_fusion), channel_id=1, source_target_pairs={{0,2},{2,4},{4,6},{6,8},{8,10},{10,12},{12,14},{14,0},{1,3},{3,5},... | collective-permute-start | bytes 1032200 | tf_op jit(solution)/shard_map/ppermute | solution.py:64
  19.8 14.4 %collective-permute-start.8 = (bf16[336,512]{1,0:T(8,128)(2,1)S(1)}, bf16[336,512]{1,0:T(8,128)(2,1)S(1)}, u32[]{:S(2)}, u32[]{:S(2)}) collective-permute-start(bf16[336,512]{1,0:T(8,128)(2,1)S(1)} %collective-permute-done.7), channel_id=1, source_target_pairs={{0,2},{2,4},{4,6},{6,8},{8,10},{10,12},{12,14},{14,0},{1,3},{3,5},... | collective-permute-start | bytes 1032200 | tf_op jit(solution)/shard_map/ppermute | solution.py:64
  20.4 16.6 %collective-permute-start.11 = (bf16[336,512]{1,0:T(8,128)(2,1)S(1)}, bf16[336,512]{1,0:T(8,128)(2,1)S(1)}, u32[]{:S(2)}, u32[]{:S(2)}) collective-permute-start(bf16[336,512]{1,0:T(8,128)(2,1)S(1)} %constant_dynamic-slice_fusion), channel_id=1, source_target_pairs={{2,0},{4,2},{6,4},{8,6},{10,8},{12,10},{14,12},{0,14},{3,1},{5,3},... | collective-permute-start | bytes 1032200 | tf_op jit(solution)/shard_map/ppermute | solution.py:66
  34.2 11.4 %collective-permute-start.9 = (bf16[336,512]{1,0:T(8,128)(2,1)S(1)}, bf16[336,512]{1,0:T(8,128)(2,1)S(1)}, u32[]{:S(2)}, u32[]{:S(2)}) collective-permute-start(bf16[336,512]{1,0:T(8,128)(2,1)S(1)} %collective-permute-done.8), channel_id=1, source_target_pairs={{0,2},{2,4},{4,6},{6,8},{8,10},{10,12},{12,14},{14,0},{1,3},{3,5},... | collective-permute-start | bytes 1032200 | tf_op jit(solution)/shard_map/ppermute | solution.py:64
  37.0 17.7 %copy-start.8 = (bf16[336,512]{1,0:T(8,128)(2,1)}, bf16[336,512]{1,0:T(8,128)(2,1)S(1)}, u32[]{:S(2)}) copy-start(bf16[336,512]{1,0:T(8,128)(2,1)S(1)} %collective-permute-done.11) | copy-start | bytes 1032196
  37.0 16.0 %collective-permute-start.12 = (bf16[336,512]{1,0:T(8,128)(2,1)S(1)}, bf16[336,512]{1,0:T(8,128)(2,1)}, u32[]{:S(2)}, u32[]{:S(2)}) collective-permute-start(bf16[336,512]{1,0:T(8,128)(2,1)S(1)} %collective-permute-done.11), channel_id=1, source_target_pairs={{2,0},{4,2},{6,4},{8,6},{10,8},{12,10},{14,12},{0,14},{3,1},{5,3},... | collective-permute-start | bytes 1032200 | tf_op jit(solution)/shard_map/ppermute | solution.py:66
  45.6 15.8 %collective-permute-start.10 = (bf16[336,512]{1,0:T(8,128)(2,1)S(1)}, bf16[336,512]{1,0:T(8,128)(2,1)}, u32[]{:S(2)}, u32[]{:S(2)}) collective-permute-start(bf16[336,512]{1,0:T(8,128)(2,1)S(1)} %collective-permute-done.9), channel_id=1, source_target_pairs={{0,2},{2,4},{4,6},{6,8},{8,10},{10,12},{12,14},{14,0},{1,3},{3,5},... | collective-permute-start | bytes 1032200 | tf_op jit(solution)/shard_map/ppermute | solution.py:64
  45.6 19.8 %copy-start.3 = (bf16[336,1024]{1,0:T(8,128)(2,1)S(1)}, bf16[336,1024]{1,0:T(8,128)(2,1)}, u32[]{:S(2)}) copy-start(bf16[336,1024]{1,0:T(8,128)(2,1)} %param.13) | copy-start | bytes 2064388
  52.9 15.6 %collective-permute-start.13 = (bf16[336,512]{1,0:T(8,128)(2,1)}, bf16[336,512]{1,0:T(8,128)(2,1)S(1)}, u32[]{:S(2)}, u32[]{:S(2)}) collective-permute-start(bf16[336,512]{1,0:T(8,128)(2,1)} %collective-permute-done.12), channel_id=1, source_target_pairs={{2,0},{4,2},{6,4},{8,6},{10,8},{12,10},{14,12},{0,14},{3,1},{5,3},... | collective-permute-start | bytes 1032200 | tf_op jit(solution)/shard_map/ppermute | solution.py:66
  70.8 14.3 %copy-start.15 = (s32[1,128]{1,0:T(1,128)S(1)}, s32[1,128]{1,0:T(1,128)}, u32[]{:S(2)}) copy-start(s32[1,128]{1,0:T(1,128)} %param.19) | copy-start | bytes 1540
  70.8 43.2 %copy-start.4 = (bf16[1,128,2048]{2,1,0:T(8,128)(2,1)S(1)}, bf16[1,128,2048]{2,1,0:T(8,128)(2,1)}, u32[]{:S(2)}) copy-start(bf16[1,128,2048]{2,1,0:T(8,128)(2,1)} %param.16) | copy-start | bytes 1572868
  70.8 44.4 %copy-start.5 = (bf16[1,128,2048]{2,1,0:T(8,128)(2,1)S(1)}, bf16[1,128,2048]{2,1,0:T(8,128)(2,1)}, u32[]{:S(2)}) copy-start(bf16[1,128,2048]{2,1,0:T(8,128)(2,1)} %param.11) | copy-start | bytes 1572868
  70.8 44.8 %copy-start.12 = (bf16[2688,16]{0,1:T(8,128)(2,1)S(1)}, bf16[2688,16]{0,1:T(8,128)(2,1)}, u32[]{:S(2)}) copy-start(bf16[2688,16]{0,1:T(8,128)(2,1)} %param.14) | copy-start | bytes 258052
  70.8 287.9 %all-reduce.4.cloned.1.call-start = ((), (), s32[]{:S(2)}) async-start(), calls=%async_computation.1 | async-start | bytes 475136 | tf_op jit(solution)/shard_map/psum | solution.py:165
  70.9 48.9 %collective-permute-start = (bf16[128,1024]{1,0:T(8,128)(2,1)}, bf16[128,1024]{1,0:T(8,128)(2,1)S(1)}, u32[]{:S(2)}, u32[]{:S(2)}) collective-permute-start(bf16[128,1024]{1,0:T(8,128)(2,1)} %bitcast.3), channel_id=1, source_target_pairs={{0,14},{1,15},{16,30},{17,31}} | collective-permute-start | bytes 786440 | tf_op jit(solution)/shard_map/ppermute | solution.py:29
  71.7 52.9 %collective-permute-start.1 = (bf16[128,1024]{1,0:T(8,128)(2,1)}, bf16[128,1024]{1,0:T(8,128)(2,1)}, u32[]{:S(2)}, u32[]{:S(2)}) collective-permute-start(bf16[128,1024]{1,0:T(8,128)(2,1)} %bitcast.3), channel_id=1, source_target_pairs={{0,12},{2,14},{1,13},{3,15},{16,28},{18,30},{17,29},{19,31}} | collective-permute-start | bytes 786440 | tf_op jit(solution)/shard_map/ppermute | solution.py:29
  73.1 54.5 %collective-permute-start.2 = (bf16[128,1024]{1,0:T(8,128)(2,1)}, bf16[128,1024]{1,0:T(8,128)(2,1)}, u32[]{:S(2)}, u32[]{:S(2)}) collective-permute-start(bf16[128,1024]{1,0:T(8,128)(2,1)} %bitcast.3), channel_id=1, source_target_pairs={{0,10},{2,12},{4,14},{1,11},{3,13},{5,15},{16,26},{18,28},{20,30},... | collective-permute-start | bytes 786440 | tf_op jit(solution)/shard_map/ppermute | solution.py:29
  83.1 45.5 %collective-permute-start.3 = (bf16[128,1024]{1,0:T(8,128)(2,1)}, bf16[128,1024]{1,0:T(8,128)(2,1)}, u32[]{:S(2)}, u32[]{:S(2)}) collective-permute-start(bf16[128,1024]{1,0:T(8,128)(2,1)} %bitcast.3), channel_id=1, source_target_pairs={{0,8},{2,10},{4,12},{6,14},{1,9},{3,11},{5,13},{7,15},{16,24},{18,... | collective-permute-start | bytes 786440 | tf_op jit(solution)/shard_map/ppermute | solution.py:29
  113.9 2.0 collective-permute-start.14
  115.9 13.6 %collective-permute-start.4 = (bf16[128,1024]{1,0:T(8,128)(2,1)}, bf16[128,1024]{1,0:T(8,128)(2,1)S(1)}, u32[]{:S(2)}, u32[]{:S(2)}) collective-permute-start(bf16[128,1024]{1,0:T(8,128)(2,1)} %bitcast.3), channel_id=1, source_target_pairs={{0,6},{2,8},{4,10},{6,12},{8,14},{1,7},{3,9},{5,11},{7,13},{9,15},... | collective-permute-start | bytes 786440 | tf_op jit(solution)/shard_map/ppermute | solution.py:29
  120.5 12.9 %collective-permute-start.5 = (bf16[128,1024]{1,0:T(8,128)(2,1)}, bf16[128,1024]{1,0:T(8,128)(2,1)S(1)}, u32[]{:S(2)}, u32[]{:S(2)}) collective-permute-start(bf16[128,1024]{1,0:T(8,128)(2,1)} %bitcast.3), channel_id=1, source_target_pairs={{0,4},{2,6},{4,8},{6,10},{8,12},{10,14},{1,5},{3,7},{5,9},{7,11},{... | collective-permute-start | bytes 786440 | tf_op jit(solution)/shard_map/ppermute | solution.py:29
  124.7 12.9 %collective-permute-start.6 = (bf16[128,1024]{1,0:T(8,128)(2,1)}, bf16[128,1024]{1,0:T(8,128)(2,1)S(1)}, u32[]{:S(2)}, u32[]{:S(2)}) collective-permute-start(bf16[128,1024]{1,0:T(8,128)(2,1)} %bitcast.3), channel_id=1, source_target_pairs={{0,2},{2,4},{4,6},{6,8},{8,10},{10,12},{12,14},{1,3},{3,5},{5,7},{... | collective-permute-start | bytes 786440 | tf_op jit(solution)/shard_map/ppermute | solution.py:29
  143.8 31.4 %collective-permute-start.22 = (bf16[128,1024]{0,1:T(8,128)(2,1)}, bf16[128,1024]{0,1:T(8,128)(2,1)}, u32[]{:S(2)}, u32[]{:S(2)}) collective-permute-start(bf16[128,1024]{0,1:T(8,128)(2,1)} %fusion.15), channel_id=1, source_target_pairs={{0,14},{1,15},{16,30},{17,31}} | collective-permute-start | bytes 786440 | tf_op jit(solution)/shard_map/ppermute | solution.py:29
  145.2 34.0 %collective-permute-start.23 = (bf16[128,1024]{0,1:T(8,128)(2,1)}, bf16[128,1024]{0,1:T(8,128)(2,1)}, u32[]{:S(2)}, u32[]{:S(2)}) collective-permute-start(bf16[128,1024]{0,1:T(8,128)(2,1)} %fusion.15), channel_id=1, source_target_pairs={{0,12},{2,14},{1,13},{3,15},{16,28},{18,30},{17,29},{19,31}} | collective-permute-start | bytes 786440 | tf_op jit(solution)/shard_map/ppermute | solution.py:29
  146.5 35.6 %collective-permute-start.24 = (bf16[128,1024]{0,1:T(8,128)(2,1)}, bf16[128,1024]{0,1:T(8,128)(2,1)}, u32[]{:S(2)}, u32[]{:S(2)}) collective-permute-start(bf16[128,1024]{0,1:T(8,128)(2,1)} %fusion.15), channel_id=1, source_target_pairs={{0,10},{2,12},{4,14},{1,11},{3,13},{5,15},{16,26},{18,28},{20,30},... | collective-permute-start | bytes 786440 | tf_op jit(solution)/shard_map/ppermute | solution.py:29
  148.8 35.1 %collective-permute-start.25 = (bf16[128,1024]{0,1:T(8,128)(2,1)}, bf16[128,1024]{0,1:T(8,128)(2,1)}, u32[]{:S(2)}, u32[]{:S(2)}) collective-permute-start(bf16[128,1024]{0,1:T(8,128)(2,1)} %fusion.15), channel_id=1, source_target_pairs={{0,8},{2,10},{4,12},{6,14},{1,9},{3,11},{5,13},{7,15},{16,24},{18,... | collective-permute-start | bytes 786440 | tf_op jit(solution)/shard_map/ppermute | solution.py:29
  155.3 30.3 %collective-permute-start.26 = (bf16[128,1024]{0,1:T(8,128)(2,1)}, bf16[128,1024]{0,1:T(8,128)(2,1)}, u32[]{:S(2)}, u32[]{:S(2)}) collective-permute-start(bf16[128,1024]{0,1:T(8,128)(2,1)} %fusion.15), channel_id=1, source_target_pairs={{0,6},{2,8},{4,10},{6,12},{8,14},{1,7},{3,9},{5,11},{7,13},{9,15},... | collective-permute-start | bytes 786440 | tf_op jit(solution)/shard_map/ppermute | solution.py:29
  169.4 25.8 %slice-start = ((s8[8388608]{0:T(1024)(128)(4,1)}), s8[4194304]{0:T(1024)(128)(4,1)S(1)}, s32[]{:S(2)}) async-start(s8[8388608]{0:T(1024)(128)(4,1)} %bitcast.141), calls=%async_computation.2 | async-start | bytes 8388608
  169.4 25.8 %slice-start.1 = ((s8[8388608]{0:T(1024)(128)(4,1)}), s8[4194304]{0:T(1024)(128)(4,1)S(1)}, s32[]{:S(2)}) async-start(s8[8388608]{0:T(1024)(128)(4,1)} %bitcast.141), calls=%async_computation.3 | async-start | bytes 8388608
  175.1 20.2 %copy-start.6 = (bf16[128,8,2,128]{3,2,1,0:T(2,128)(2,1)S(1)}, bf16[128,8,2,128]{3,2,1,0:T(2,128)(2,1)}, u32[]{:S(2)}) copy-start(bf16[128,8,2,128]{3,2,1,0:T(2,128)(2,1)} %reshape_squeeze.7) | copy-start | bytes 1572868
  175.2 15.9 %collective-permute-start.27 = (bf16[128,1024]{0,1:T(8,128)(2,1)}, bf16[128,1024]{0,1:T(8,128)(2,1)S(1)}, u32[]{:S(2)}, u32[]{:S(2)}) collective-permute-start(bf16[128,1024]{0,1:T(8,128)(2,1)} %fusion.15), channel_id=1, source_target_pairs={{0,4},{2,6},{4,8},{6,10},{8,12},{10,14},{1,5},{3,7},{5,9},{7,11},{... | collective-permute-start | bytes 786440 | tf_op jit(solution)/shard_map/ppermute | solution.py:29
  179.1 13.5 %collective-permute-start.28 = (bf16[128,1024]{0,1:T(8,128)(2,1)}, bf16[128,1024]{0,1:T(8,128)(2,1)S(1)}, u32[]{:S(2)}, u32[]{:S(2)}) collective-permute-start(bf16[128,1024]{0,1:T(8,128)(2,1)} %fusion.15), channel_id=1, source_target_pairs={{0,2},{2,4},{4,6},{6,8},{8,10},{10,12},{12,14},{1,3},{3,5},{5,7},{... | collective-permute-start | bytes 786440 | tf_op jit(solution)/shard_map/ppermute | solution.py:29
  182.1 18.5 %collective-permute-start.21 = (bf16[128,1024]{0,1:T(8,128)(2,1)S(1)}, bf16[128,1024]{0,1:T(8,128)(2,1)S(1)}, u32[]{:S(2)}, u32[]{:S(2)}) collective-permute-start(bf16[128,1024]{0,1:T(8,128)(2,1)S(1)} %bitcast.161), channel_id=1, source_target_pairs={{14,0},{15,1},{30,16},{31,17}} | collective-permute-start | bytes 786440 | tf_op jit(solution)/shard_map/ppermute | solution.py:29
  183.9 19.6 %collective-permute-start.20 = (bf16[128,1024]{0,1:T(8,128)(2,1)S(1)}, bf16[128,1024]{0,1:T(8,128)(2,1)S(1)}, u32[]{:S(2)}, u32[]{:S(2)}) collective-permute-start(bf16[128,1024]{0,1:T(8,128)(2,1)S(1)} %bitcast.160), channel_id=1, source_target_pairs={{12,0},{14,2},{13,1},{15,3},{28,16},{30,18},{29,17},{31,19}} | collective-permute-start | bytes 786440 | tf_op jit(solution)/shard_map/ppermute | solution.py:29
  185.6 24.5 %collective-permute-start.19 = (bf16[128,1024]{0,1:T(8,128)(2,1)S(1)}, bf16[128,1024]{0,1:T(8,128)(2,1)S(1)}, u32[]{:S(2)}, u32[]{:S(2)}) collective-permute-start(bf16[128,1024]{0,1:T(8,128)(2,1)S(1)} %bitcast.159), channel_id=1, source_target_pairs={{10,0},{12,2},{14,4},{11,1},{13,3},{15,5},{26,16},{28,18},{30,20},... | collective-permute-start | bytes 786440 | tf_op jit(solution)/shard_map/ppermute | solution.py:29
  191.1 19.2 %collective-permute-start.18 = (bf16[128,1024]{0,1:T(8,128)(2,1)S(1)}, bf16[128,1024]{0,1:T(8,128)(2,1)S(1)}, u32[]{:S(2)}, u32[]{:S(2)}) collective-permute-start(bf16[128,1024]{0,1:T(8,128)(2,1)S(1)} %bitcast.158), channel_id=1, source_target_pairs={{8,0},{10,2},{12,4},{14,6},{9,1},{11,3},{13,5},{15,7},{24,16},{26,... | collective-permute-start | bytes 786440 | tf_op jit(solution)/shard_map/ppermute | solution.py:29
  192.6 37.2 %collective-permute-start.17 = (bf16[128,1024]{0,1:T(8,128)(2,1)S(1)}, bf16[128,1024]{0,1:T(8,128)(2,1)S(1)}, u32[]{:S(2)}, u32[]{:S(2)}) collective-permute-start(bf16[128,1024]{0,1:T(8,128)(2,1)S(1)} %bitcast.157), channel_id=1, source_target_pairs={{6,0},{8,2},{10,4},{12,6},{14,8},{7,1},{9,3},{11,5},{13,7},{15,9},... | collective-permute-start | bytes 786440 | tf_op jit(solution)/shard_map/ppermute | solution.py:29
  200.6 30.7 %collective-permute-start.16 = (bf16[128,1024]{0,1:T(8,128)(2,1)S(1)}, bf16[128,1024]{0,1:T(8,128)(2,1)S(1)}, u32[]{:S(2)}, u32[]{:S(2)}) collective-permute-start(bf16[128,1024]{0,1:T(8,128)(2,1)S(1)} %bitcast.156), channel_id=1, source_target_pairs={{4,0},{6,2},{8,4},{10,6},{12,8},{14,10},{5,1},{7,3},{9,5},{11,7},{... | collective-permute-start | bytes 786440 | tf_op jit(solution)/shard_map/ppermute | solution.py:29
  203.5 27.8 %collective-permute-start.15 = (bf16[128,1024]{0,1:T(8,128)(2,1)S(1)}, bf16[128,1024]{0,1:T(8,128)(2,1)S(1)}, u32[]{:S(2)}, u32[]{:S(2)}) collective-permute-start(bf16[128,1024]{0,1:T(8,128)(2,1)S(1)} %bitcast.155), channel_id=1, source_target_pairs={{2,0},{4,2},{6,4},{8,6},{10,8},{12,10},{14,12},{3,1},{5,3},{7,5},{... | collective-permute-start | bytes 786440 | tf_op jit(solution)/shard_map/ppermute | solution.py:29
  237.9 15.8 %collective-permute-start.35 = (bf16[128,1024]{1,0:T(8,128)(2,1)}, bf16[128,1024]{1,0:T(8,128)(2,1)S(1)}, u32[]{:S(2)}, u32[]{:S(2)}) collective-permute-start(bf16[128,1024]{1,0:T(8,128)(2,1)} %copy.53), channel_id=1, source_target_pairs={{14,0},{15,1},{30,16},{31,17}} | collective-permute-start | bytes 786440 | tf_op jit(solution)/shard_map/ppermute | solution.py:29
  240.3 15.3 %collective-permute-start.34 = (bf16[128,1024]{1,0:T(8,128)(2,1)}, bf16[128,1024]{1,0:T(8,128)(2,1)S(1)}, u32[]{:S(2)}, u32[]{:S(2)}) collective-permute-start(bf16[128,1024]{1,0:T(8,128)(2,1)} %copy.52), channel_id=1, source_target_pairs={{12,0},{14,2},{13,1},{15,3},{28,16},{30,18},{29,17},{31,19}} | collective-permute-start | bytes 786440 | tf_op jit(solution)/shard_map/ppermute | solution.py:29
  242.8 20.1 %collective-permute-start.33 = (bf16[128,1024]{1,0:T(8,128)(2,1)}, bf16[128,1024]{1,0:T(8,128)(2,1)S(1)}, u32[]{:S(2)}, u32[]{:S(2)}) collective-permute-start(bf16[128,1024]{1,0:T(8,128)(2,1)} %copy.51), channel_id=1, source_target_pairs={{10,0},{12,2},{14,4},{11,1},{13,3},{15,5},{26,16},{28,18},{30,20},... | collective-permute-start | bytes 786440 | tf_op jit(solution)/shard_map/ppermute | solution.py:29
  246.8 16.1 %collective-permute-start.32 = (bf16[128,1024]{1,0:T(8,128)(2,1)}, bf16[128,1024]{1,0:T(8,128)(2,1)S(1)}, u32[]{:S(2)}, u32[]{:S(2)}) collective-permute-start(bf16[128,1024]{1,0:T(8,128)(2,1)} %copy.50), channel_id=1, source_target_pairs={{8,0},{10,2},{12,4},{14,6},{9,1},{11,3},{13,5},{15,7},{24,16},{26,... | collective-permute-start | bytes 786440 | tf_op jit(solution)/shard_map/ppermute | solution.py:29
  249.0 29.1 %collective-permute-start.31 = (bf16[128,1024]{1,0:T(8,128)(2,1)}, bf16[128,1024]{1,0:T(8,128)(2,1)}, u32[]{:S(2)}, u32[]{:S(2)}) collective-permute-start(bf16[128,1024]{1,0:T(8,128)(2,1)} %copy.49), channel_id=1, source_target_pairs={{6,0},{8,2},{10,4},{12,6},{14,8},{7,1},{9,3},{11,5},{13,7},{15,9},... | collective-permute-start | bytes 786440 | tf_op jit(solution)/shard_map/ppermute | solution.py:29
  253.7 29.6 %collective-permute-start.30 = (bf16[128,1024]{1,0:T(8,128)(2,1)}, bf16[128,1024]{1,0:T(8,128)(2,1)S(1)}, u32[]{:S(2)}, u32[]{:S(2)}) collective-permute-start(bf16[128,1024]{1,0:T(8,128)(2,1)} %copy.48), channel_id=1, source_target_pairs={{4,0},{6,2},{8,4},{10,6},{12,8},{14,10},{5,1},{7,3},{9,5},{11,7},{... | collective-permute-start | bytes 786440 | tf_op jit(solution)/shard_map/ppermute | solution.py:29
  255.6 27.7 %collective-permute-start.29 = (bf16[128,1024]{1,0:T(8,128)(2,1)}, bf16[128,1024]{1,0:T(8,128)(2,1)S(1)}, u32[]{:S(2)}, u32[]{:S(2)}) collective-permute-start(bf16[128,1024]{1,0:T(8,128)(2,1)} %copy.46), channel_id=1, source_target_pairs={{2,0},{4,2},{6,4},{8,6},{10,8},{12,10},{14,12},{3,1},{5,3},{7,5},{... | collective-permute-start | bytes 786440 | tf_op jit(solution)/shard_map/ppermute | solution.py:29
  (10 other events, 76.5 us)
Sparse Core Ops, SparseCore 0:
  71.0 20.3 all-gather.1
  253.4 105.3 all-reduce.3
